TPU v7x, 32 devices: a whole 2x2x4 slice. The times are simulated.
32 devices in a mesh: comp: 4 (over x, core), blk: 8 (over z, y).
Axes of the slice: x: 2, y: 2, z: 4, core: 2. Of those that a mesh axis runs over, the one named last changes fastest.
Arguments:
- start_modes: float32 [4, 32768, 256], P('comp', 'blk')
- stiff_diag: float32 [4, 256, 128, 128], P('comp', 'blk')
- stiff_off: float32 [4, 256, 128, 128], P('comp', 'blk'), may hold values from -0.625 to 0.625
- mass_blocks: float32 [4, 256, 128, 128], P('comp', 'blk')
- coupling: float32 [4, 256, 128, 128], P('comp', 'blk'), may hold values from -6 to 6
- interface_block: int32 [4, 256], P('comp', 'blk'), may hold values from 0 to 8
- global_iface: int32 [4, 8], P('comp'), may hold values from 0 to 15
Outputs:
- modes: float32 [4, 32768, 256], P('comp', 'blk')
- reduced_stiffness: float32 [4, 256, 256], P('comp')
- assembled: float32 [16, 128, 128], P('comp')
All inputs are finite; a program needn't handle non-finite values.
Results may differ from a plain program's by a relative error of at most 0.0003.
Values sent between devices are 32-bit elements; how exact they have to be, the bound alone decides.
No kernel may reach another device: no remote copies, remote signals or barrier semaphores. Data moves between devices by JAX's collectives and lax.ppermute only.
A program may use at most 128 MiB of HBM per device.

v0:
```python
import jax
import jax.numpy as jnp
from jax import lax
from jax.sharding import PartitionSpec as P

ITERS = 2
GIFC = 4


highest = lax.Precision.HIGHEST
step_size = 0.15


def passed_along(value, axis, steps):
    count = lax.axis_size(axis)
    initial, last = (max(0, -steps), min(count, count - steps))
    return lax.ppermute(value, axis, [(source, source + steps) for source in range(initial, last)])


def extended_2(block, sides, width):
    for axis, dim in sides:
        count = lax.axis_size(axis)
        forward = [(i, i + 1) for i in range(count - 1)]
        backward = [(target, source) for source, target in forward]
        low = lax.ppermute(
            lax.slice_in_dim(block, block.shape[dim] - width, None, axis=dim), axis, forward
        )
        high = lax.ppermute(lax.slice_in_dim(block, 0, width, axis=dim), axis, backward)
        block = jnp.concatenate([low, block, high], axis=dim)
    return block


def block_product(blocks, vectors):
    return jnp.einsum("bij,bjm->bim", blocks, vectors, precision=highest)


def lower_inverse(matrix):
    factor = jnp.linalg.cholesky(matrix)
    unit_matrix = jnp.eye(matrix.shape[0], dtype=matrix.dtype)
    return lax.linalg.triangular_solve(factor, unit_matrix, left_side=True, lower=True)


def local(start_modes, stiff_diag, stiff_off, mass_blocks, coupling, interface_block, global_iface):
    start_flat = start_modes[0]
    stiff_self = stiff_diag[0]
    stiff_link = stiff_off[0]
    mass_self = mass_blocks[0]
    coupling_blocks = coupling[0]
    interface_ids = interface_block[0]
    global_ids = global_iface[0]
    row_count, mode_count = start_flat.shape
    blocks_dev = stiff_self.shape[0]
    block_size = stiff_self.shape[1]
    dof_count = row_count * lax.axis_size("blk")
    link_next = passed_along(stiff_link[:1], "blk", -1)
    link_after = jnp.concatenate([stiff_link[1:], link_next], 0)

    def stiff_apply(vectors):
        padded = extended_2(vectors, (("blk", 0),), block_size)
        extended = padded.reshape(blocks_dev + 2, block_size, mode_count)
        result = block_product(stiff_self, extended[1 : blocks_dev + 1]) + block_product(
            stiff_link, extended[:blocks_dev]
        )
        result = result + jnp.einsum("bji,bjm->bim", link_after, extended[2:], precision=highest)
        return result.reshape(row_count, mode_count)

    def gram_matrix(left, right):
        return jnp.dot(left.T, right, precision=highest) / dof_count

    basis = start_flat
    stiff_basis = stiff_apply(basis)
    reduced = jnp.zeros((mode_count, mode_count), jnp.float32)
    for sweep in range(ITERS):
        filtered = basis - step_size * stiff_basis
        mass_part = block_product(
            mass_self, filtered.reshape(blocks_dev, block_size, mode_count)
        ).reshape(row_count, mode_count)
        stiff_part = stiff_apply(filtered)
        mass_gram, stiff_gram = lax.psum(
            (gram_matrix(filtered, mass_part), gram_matrix(filtered, stiff_part)), "blk"
        )
        factor_inv = lower_inverse(mass_gram)
        basis = jnp.dot(filtered, factor_inv.T, precision=highest)
        if sweep + 1 < ITERS:
            stiff_basis = jnp.dot(stiff_part, factor_inv.T, precision=highest)
        reduced = jnp.dot(
            jnp.dot(factor_inv, stiff_gram, precision=highest), factor_inv.T, precision=highest
        )
    iface_count = global_ids.shape[0]
    block_terms = jnp.einsum(
        "bkm,bkl->bml",
        basis.reshape(blocks_dev, block_size, mode_count),
        coupling_blocks,
        precision=highest,
    )
    onehot = (interface_ids[:, None] == jnp.arange(iface_count, dtype=jnp.int32)[None, :]).astype(
        jnp.float32
    )
    coupling_term = (
        jnp.einsum("bj,bml->mjl", onehot, block_terms, precision=highest) / dof_count**0.5
    )
    reduced_inv = lower_inverse(reduced)
    shared = lax.psum(coupling_term, "blk")
    scaled = jnp.einsum("nm,mjl->njl", reduced_inv, shared, precision=highest)
    condensed = jnp.einsum("njk,njl->jkl", scaled, scaled, precision=highest)
    global_count = GIFC * lax.axis_size("comp")
    placed = (global_ids[:, None] == jnp.arange(global_count, dtype=jnp.int32)[None, :]).astype(
        jnp.float32
    )
    dense_sum = jnp.einsum("jg,jkl->gkl", placed, condensed, precision=highest)
    owned = lax.psum_scatter(dense_sum, "comp", scatter_dimension=0, tiled=True)
    return (basis[None], reduced[None], owned)


def solution(mesh):
    in_specs = (
        P("comp", "blk", None),
        P("comp", "blk", None, None),
        P("comp", "blk", None, None),
        P("comp", "blk", None, None),
        P("comp", "blk", None, None),
        P("comp", "blk"),
        P("comp", None),
    )
    out_specs = (P("comp", "blk", None), P("comp", None, None), P("comp", None, None))
    return jax.shard_map(local, mesh=mesh, in_specs=in_specs, out_specs=out_specs, check_vma=False)
```

profile of v0, /device:TPU:0, one launch (start us, length us, event | category | flops | bytes accessed | tf_op | source)
XLA Modules:
  0.0 577.0 jit_solution(13938098637092562167)
XLA Ops:
  8.4 4.9 collective-permute-start
  16.8 8.2 %fusion.23 = f32[32,128,256]{2,1,0:T(8,128)} fusion(f32[32,128,256]{2,1,0:T(8,128)} %bitcast.199, f32[1,32,128,128]{3,2,1,0:T(8,128)S(1)} %copy-done), kind=kOutput, calls=%fused_computation.42 | convolution fusion | flops 1610612736 | bytes 10485760 | tf_op jit(solution)/shard_map/bij,bjm->bim/dot_general | solution.py:34
  25.0 1.5 slice.129
  26.5 3.2 copy.45
  29.7 4.1 pad_maximum_fusion.4
  33.8 5.3 fusion.17
  39.1 6.6 %fusion.4 = f32[32,128,256]{2,1,0:T(8,128)S(1)} fusion(f32[32,128,256]{2,1,0:T(8,128)} %fusion.23, f32[32,256,128]{1,2,0:T(8,128)} %fusion.17, f32[32,128,256]{2,1,0:T(8,128)S(1)} %bitcast.214, f32[1,128,128]{1,2,0:T(8,128)S(1)} %collective-permute-done.1, f32[31,128,128]{1,2,0:T(8,128)S(1)} %bitcast.204), kind=kOutput, calls=%fused_computation.22 | convolution fusion | flops 1614282752 | bytes 18874368 | tf_op jit(solution)/shard_map/bji,bjm->bim/dot_general | solution.py:64
  46.6 5.9 %fusion.21 = f32[32,256,128]{1,2,0:T(8,128)} fusion(f32[1,32,128,128]{3,2,1,0:T(8,128)S(1)} %copy-done, f32[32,128,256]{2,1,0:T(8,128)S(1)} %bitcast.201, f32[32,128,256]{2,1,0:T(8,128)S(1)} %fusion.4), kind=kOutput, calls=%fused_computation.40 | convolution fusion | flops 1611661312 | bytes 14680064 | tf_op jit(solution)/shard_map/bij,bjm->bim/dot_general | solution.py:34
  52.6 4.2 fusion.11
  57.3 5.2 collective-permute-start.3
  63.8 7.5 %fusion.33 = f32[256,256]{0,1:T(8,128)} fusion(f32[4096,256]{1,0:T(8,128)S(1)} %bitcast.207, f32[1,4096,256]{2,1,0:T(8,128)S(1)} %bitcast_subtract_fusion), kind=kOutput, calls=%fused_computation.48 | convolution fusion | flops 3221291008 | bytes 8650752 | tf_op jit(solution)/shard_map/dot_general | solution.py:68
  71.5 4.1 pad_maximum_fusion.2
  75.6 4.4 fusion.15
  80.1 6.0 %bitcast_add_fusion.1 = f32[32,128,256]{2,1,0:T(8,128)} fusion(f32[32,256,128]{1,2,0:T(8,128)S(1)} %copy-done.14, f32[32,256,128]{1,2,0:T(8,128)S(1)} %fusion.15, f32[32,128,256]{2,1,0:T(8,128)S(1)} %bitcast.217, f32[1,128,128]{1,2,0:T(8,128)S(1)} %collective-permute-done.1, f32[31,128,128]{1,2,0:T(8,128)S(1)} %bitcast.205), kind=kOutput, calls=%fused_computation.15 | convolution fusion | flops 1613234176 | bytes 18874368 | tf_op jit(solution)/shard_map/bji,bjm->bim/dot_general | solution.py:64
  86.1 59.6 %all-reduce.6.cloned.1.call-done = f32[256,256]{0,1:T(8,128)} async-done(((f32[256,256]{0,1:T(8,128)}), f32[256,256]{0,1:T(8,128)}) %all-reduce.6.cloned.1.call-update) | async-done | bytes 262160 | tf_op jit(solution)/shard_map/psum | solution.py:79
  147.8 11.7 %cholesky.172 = f32[128,128]{1,0:T(8,128)S(1)} custom-call(f32[128,128]{1,0:T(8,128)S(1)} %cholesky.270), custom_call_target="Cholesky" | custom-call | tf_op jit(solution)/shard_map/jit(cholesky)/cholesky | solution.py:38
  159.6 9.8 %custom-call.15 = f32[1,128,128]{1,2,0:T(8,128)S(1)} custom-call(f32[1,128,128]{2,1,0:T(8,128)S(1)} %get-tuple-element.86), custom_call_target="InvertDiagBlocksLowerTriangular" | custom-call | tf_op jit(solution)/shard_map/jit(cholesky)/cholesky | solution.py:38
  169.9 11.7 %cholesky.189 = f32[128,128]{1,0:T(8,128)S(1)} custom-call(f32[128,128]{1,0:T(8,128)S(1)} %convolution_subtract_fusion.5), custom_call_target="Cholesky" | custom-call | tf_op jit(solution)/shard_map/jit(cholesky)/cholesky | solution.py:38
  183.6 3.8 while.6
  187.5 20.1 %custom-call.16 = f32[2,128,128]{1,2,0:T(8,128)S(1)} custom-call(f32[2,128,128]{2,1,0:T(8,128)S(1)} %get-tuple-element.25), custom_call_target="InvertDiagBlocksLowerTriangular" | custom-call | tf_op jit(solution)/shard_map/triangular_solve/custom-call.0 | solution.py:40
  208.5 5.4 fusion.46
  214.0 3.6 fusion
  217.6 5.5 fusion.19
  223.1 4.6 fusion.9
  227.7 2.7 collective-permute-start.5
  231.7 7.8 %convolution_multiply_fusion.2 = f32[256,256]{0,1:T(8,128)} fusion(f32[4096,256]{1,0:T(8,128)S(1)} %fusion, f32[4096,256]{1,0:T(8,128)S(1)} %bitcast.215), kind=kOutput, calls=%fused_computation.50 | convolution fusion | flops 3221291008 | bytes 8650752 | tf_op jit(solution)/shard_map/dot_general | solution.py:68
  239.6 4.1 pad_maximum_fusion
  243.7 5.3 fusion.13
  249.0 6.6 %bitcast_add_fusion = f32[32,128,256]{2,1,0:T(8,128)S(1)} fusion(f32[32,256,128]{1,2,0:T(8,128)S(1)} %copy-done.15, f32[32,256,128]{1,2,0:T(8,128)} %fusion.13, f32[32,128,256]{2,1,0:T(8,128)S(1)} %bitcast.216, f32[1,128,128]{1,2,0:T(8,128)S(1)} %collective-permute-done.1, f32[31,128,128]{1,2,0:T(8,128)S(1)} %bitcast.206), kind=kOutput, calls=%fused_computation.14 | convolution fusion | flops 1613234176 | bytes 18874368 | tf_op jit(solution)/shard_map/bji,bjm->bim/dot_general | solution.py:64
  255.6 7.6 %convolution_multiply_fusion.1 = f32[256,256]{0,1:T(8,128)} fusion(f32[4096,256]{1,0:T(8,128)S(1)} %copy-done.2, f32[4096,256]{1,0:T(8,128)S(1)} %bitcast.218), kind=kOutput, calls=%fused_computation.49 | convolution fusion | flops 3221291008 | bytes 8650752 | tf_op jit(solution)/shard_map/dot_general | solution.py:68
  263.3 48.8 %all-reduce.8.cloned.1.call-done = f32[256,256]{0,1:T(8,128)} async-done(((f32[256,256]{0,1:T(8,128)}), f32[256,256]{0,1:T(8,128)}) %all-reduce.8.cloned.1.call-update) | async-done | bytes 262160 | tf_op jit(solution)/shard_map/psum | solution.py:79
  314.1 11.7 %cholesky.206 = f32[128,128]{1,0:T(8,128)S(1)} custom-call(f32[128,128]{1,0:T(8,128)S(1)} %cholesky.273), custom_call_target="Cholesky" | custom-call | tf_op jit(solution)/shard_map/jit(cholesky)/cholesky | solution.py:38
  325.9 9.9 %custom-call.17 = f32[1,128,128]{1,2,0:T(8,128)S(1)} custom-call(f32[1,128,128]{2,1,0:T(8,128)S(1)} %get-tuple-element.82), custom_call_target="InvertDiagBlocksLowerTriangular" | custom-call | tf_op jit(solution)/shard_map/jit(cholesky)/cholesky | solution.py:38
  336.3 11.7 %cholesky.223 = f32[128,128]{1,0:T(8,128)S(1)} custom-call(f32[128,128]{1,0:T(8,128)S(1)} %convolution_subtract_fusion.4), custom_call_target="Cholesky" | custom-call | tf_op jit(solution)/shard_map/jit(cholesky)/cholesky | solution.py:38
  350.6 3.8 while.7
  354.4 19.7 %custom-call.18 = f32[2,128,128]{1,2,0:T(8,128)S(1)} custom-call(f32[2,128,128]{2,1,0:T(8,128)S(1)} %get-tuple-element.26), custom_call_target="InvertDiagBlocksLowerTriangular" | custom-call | tf_op jit(solution)/shard_map/triangular_solve/custom-call.0 | solution.py:40
  375.0 5.8 %fusion.49 = f32[4096,256]{1,0:T(8,128)S(1)} fusion(f32[4096,256]{1,0:T(8,128)} %copy-done.1, f32[128,256]{1,0:T(8,128)S(1)} %fusion.61, f32[128,256]{1,0:T(8,128)S(1)} %fusion.52), kind=kOutput, calls=%fused_computation.81 | convolution fusion | flops 3221291008 | bytes 8650752 | tf_op jit(solution)/shard_map/dot_general | solution.py:83
  380.8 7.3 %fusion.7 = f32[32,256,128]{2,1,0:T(8,128)S(1)} fusion(f32[32,128,256]{2,1,0:T(8,128)S(1)} %bitcast.211, f32[1,32,128,128]{3,2,1,0:T(8,128)S(1)} %copy-done.19), kind=kOutput, calls=%fused_computation.26 | convolution fusion | flops 1610612736 | bytes 10485760 | tf_op jit(solution)/shard_map/bkm,bkl->bml/dot_general | solution.py:90
  388.2 4.8 fusion.30
  393.5 82.7 %all-reduce.10.cloned.1.call-done = (f32[256,256]{0,1:T(8,128)}, f32[256,8,128]{2,1,0:T(8,128)}) async-done(((f32[256,256]{0,1:T(8,128)}, f32[256,8,128]{2,1,0:T(8,128)}), (f32[256,256]{0,1:T(8,128)}, f32[256,8,128]{2,1,0:T(8,128)})) %all-reduce.10.cloned.1.call-update) | async-done | bytes 1310736 | tf_op jit(solution)/shard_map/psum | solution.py:79
  478.2 11.7 %cholesky.240 = f32[128,128]{1,0:T(8,128)S(1)} custom-call(f32[128,128]{1,0:T(8,128)S(1)} %cholesky.276), custom_call_target="Cholesky" | custom-call | tf_op jit(solution)/shard_map/jit(cholesky)/cholesky | solution.py:38
  490.0 9.8 %custom-call.19 = f32[1,128,128]{1,2,0:T(8,128)S(1)} custom-call(f32[1,128,128]{2,1,0:T(8,128)S(1)} %get-tuple-element.78), custom_call_target="InvertDiagBlocksLowerTriangular" | custom-call | tf_op jit(solution)/shard_map/jit(cholesky)/cholesky | solution.py:38
  500.3 11.7 %cholesky.257 = f32[128,128]{1,0:T(8,128)S(1)} custom-call(f32[128,128]{1,0:T(8,128)S(1)} %convolution_subtract_fusion.3), custom_call_target="Cholesky" | custom-call | tf_op jit(solution)/shard_map/jit(cholesky)/cholesky | solution.py:38
  514.8 4.2 while.8
  519.0 19.7 %custom-call.20 = f32[2,128,128]{1,2,0:T(8,128)S(1)} custom-call(f32[2,128,128]{2,1,0:T(8,128)S(1)} %get-tuple-element.27), custom_call_target="InvertDiagBlocksLowerTriangular" | custom-call | tf_op jit(solution)/shard_map/triangular_solve/custom-call.0 | solution.py:40
  539.6 2.4 fusion.36
  542.0 1.9 fusion.91
  546.1 24.2 %reduce-scatter.2.cloned.1.call-done = f32[4,128,128]{2,1,0:T(8,128)} async-done(((f32[16,128,128]{2,1,0:T(8,128)}), f32[4,128,128]{2,1,0:T(8,128)}) %reduce-scatter.2.cloned.1.call-update) | async-done | bytes 262160 | tf_op jit(solution)/shard_map/reduce_scatter | solution.py:111
  (139 shorter events, 37.1 us)
Async XLA Ops:
  7.2 9.6 %copy-start = (f32[1,32,128,128]{3,2,1,0:T(8,128)S(1)}, f32[1,32,128,128]{3,2,1,0:T(8,128)}, u32[]{:S(2)}) copy-start(f32[1,32,128,128]{3,2,1,0:T(8,128)} %param.11) | copy-start | bytes 6291460
  7.2 138.6 %all-reduce.6.cloned.1.call-start = ((), (), s32[]{:S(2)}) async-start(), calls=%async_computation.1 | async-start | bytes 524288 | tf_op jit(solution)/shard_map/psum | solution.py:79
  8.4 21.3 %collective-permute-start = (f32[128,256]{1,0:T(8,128)S(1)}, f32[128,256]{1,0:T(8,128)S(1)}, u32[]{:S(2)}, u32[]{:S(2)}) collective-permute-start(f32[128,256]{1,0:T(8,128)S(1)} %get-tuple-element.74), channel_id=1, source_target_pairs={{0,1},{1,2},{2,3},{3,4},{4,5},{5,6},{6,7},{8,9},{9,10},{10,11},{11... | collective-permute-start | bytes 393224 | tf_op jit(solution)/shard_map/ppermute | solution.py:25
  13.2 16.5 %collective-permute-start.2 = (f32[128,256]{1,0:T(8,128)S(1)}, f32[128,256]{1,0:T(8,128)S(1)}, u32[]{:S(2)}, u32[]{:S(2)}) collective-permute-start(f32[128,256]{1,0:T(8,128)S(1)} %get-tuple-element.73), channel_id=1, source_target_pairs={{1,0},{2,1},{3,2},{4,3},{5,4},{6,5},{7,6},{9,8},{10,9},{11,10},{12... | collective-permute-start | bytes 393224 | tf_op jit(solution)/shard_map/ppermute | solution.py:28
  15.5 23.6 %collective-permute-start.1 = (f32[1,128,128]{1,2,0:T(8,128)S(1)}, f32[1,128,128]{1,2,0:T(8,128)S(1)}, u32[]{:S(2)}, u32[]{:S(2)}) collective-permute-start(f32[1,128,128]{1,2,0:T(8,128)S(1)} %bitcast.220), channel_id=1, source_target_pairs={{1,0},{2,1},{3,2},{4,3},{5,4},{6,5},{7,6},{9,8},{10,9},{11,10},{12... | collective-permute-start | bytes 196616 | tf_op jit(solution)/shard_map/ppermute | solution.py:17
  16.8 8.2 %copy-start.5 = (f32[1,32,128,128]{3,2,1,0:T(8,128)S(1)}, f32[1,32,128,128]{3,2,1,0:T(8,128)}, u32[]{:S(2)}) copy-start(f32[1,32,128,128]{3,2,1,0:T(8,128)} %param.12) | copy-start | bytes 6291460
  29.7 4.1 copy-start.6
  33.8 5.3 copy-start.9
  39.1 6.7 %copy-start.3 = (f32[1,4096,256]{2,1,0:T(8,128)S(1)}, f32[1,4096,256]{2,1,0:T(8,128)}, u32[]{:S(2)}) copy-start(f32[1,4096,256]{2,1,0:T(8,128)} %param.10) | copy-start | bytes 12582916
  46.6 10.7 %copy-start.4 = (f32[4096,256]{1,0:T(8,128)}, f32[4096,256]{1,0:T(8,128)S(1)}, u32[]{:S(2)}) copy-start(f32[4096,256]{1,0:T(8,128)S(1)} %bitcast_subtract_fusion.1) | copy-start | bytes 12582916
  46.6 5.9 %copy-start.16 = (f32[1,32,128,128]{3,2,1,0:T(8,128)S(1)}, f32[1,32,128,128]{3,2,1,0:T(8,128)}, u32[]{:S(2)}) copy-start(f32[1,32,128,128]{3,2,1,0:T(8,128)} %param.13) | copy-start | bytes 6291460
  57.3 14.2 %collective-permute-start.3 = (f32[128,256]{1,0:T(8,128)S(1)}, f32[128,256]{1,0:T(8,128)S(1)}, u32[]{:S(2)}, u32[]{:S(2)}) collective-permute-start(f32[128,256]{1,0:T(8,128)S(1)} %get-tuple-element.70), channel_id=1, source_target_pairs={{0,1},{1,2},{2,3},{3,4},{4,5},{5,6},{6,7},{8,9},{9,10},{10,11},{11... | collective-permute-start | bytes 393224 | tf_op jit(solution)/shard_map/ppermute | solution.py:25
  62.5 9.0 %collective-permute-start.4 = (f32[128,256]{1,0:T(8,128)S(1)}, f32[128,256]{1,0:T(8,128)S(1)}, u32[]{:S(2)}, u32[]{:S(2)}) collective-permute-start(f32[128,256]{1,0:T(8,128)S(1)} %get-tuple-element.69), channel_id=1, source_target_pairs={{1,0},{2,1},{3,2},{4,3},{5,4},{6,5},{7,6},{9,8},{10,9},{11,10},{12... | collective-permute-start | bytes 393224 | tf_op jit(solution)/shard_map/ppermute | solution.py:28
  71.3 240.8 %all-reduce.8.cloned.1.call-start = ((), (), s32[]{:S(2)}) async-start(), calls=%async_computation.2 | async-start | bytes 524288 | tf_op jit(solution)/shard_map/psum | solution.py:79
  71.5 4.1 copy-start.7
  75.6 4.5 copy-start.10
  75.6 4.5 copy-start.14
  208.5 5.5 copy-start.13
  217.6 14.1 %copy-start.1 = (f32[4096,256]{1,0:T(8,128)}, f32[4096,256]{1,0:T(8,128)S(1)}, u32[]{:S(2)}) copy-start(f32[4096,256]{1,0:T(8,128)S(1)} %fusion) | copy-start | bytes 12582916
  217.6 5.5 copy-start.17
  227.7 11.8 %collective-permute-start.5 = (f32[128,256]{1,0:T(8,128)S(1)}, f32[128,256]{1,0:T(8,128)S(1)}, u32[]{:S(2)}, u32[]{:S(2)}) collective-permute-start(f32[128,256]{1,0:T(8,128)S(1)} %get-tuple-element.66), channel_id=1, source_target_pairs={{0,1},{1,2},{2,3},{3,4},{4,5},{5,6},{6,7},{8,9},{9,10},{10,11},{11... | collective-permute-start | bytes 393224 | tf_op jit(solution)/shard_map/ppermute | solution.py:25
  230.4 9.2 %collective-permute-start.6 = (f32[128,256]{1,0:T(8,128)S(1)}, f32[128,256]{1,0:T(8,128)S(1)}, u32[]{:S(2)}, u32[]{:S(2)}) collective-permute-start(f32[128,256]{1,0:T(8,128)S(1)} %get-tuple-element.65), channel_id=1, source_target_pairs={{1,0},{2,1},{3,2},{4,3},{5,4},{6,5},{7,6},{9,8},{10,9},{11,10},{12... | collective-permute-start | bytes 393224 | tf_op jit(solution)/shard_map/ppermute | solution.py:28
  239.5 236.7 %all-reduce.10.cloned.1.call-start = ((), (), s32[]{:S(2)}) async-start(), calls=%async_computation.4 | async-start | bytes 2621440 | tf_op jit(solution)/shard_map/psum | solution.py:79
  239.5 4.1 copy-start.8
  243.6 5.3 copy-start.11
  243.7 5.3 copy-start.15
  249.0 6.7 %copy-start.2 = (f32[4096,256]{1,0:T(8,128)S(1)}, f32[4096,256]{1,0:T(8,128)}, u32[]{:S(2)}) copy-start(f32[4096,256]{1,0:T(8,128)} %copy-done.1) | copy-start | bytes 12582916
  375.0 5.8 %copy-start.19 = (f32[1,32,128,128]{3,2,1,0:T(8,128)S(1)}, f32[1,32,128,128]{3,2,1,0:T(8,128)}, u32[]{:S(2)}) copy-start(f32[1,32,128,128]{3,2,1,0:T(8,128)} %param.14) | copy-start | bytes 6291460
  380.8 7.3 %copy-start.12 = (f32[4096,256]{1,0:T(8,128)}, f32[4096,256]{1,0:T(8,128)S(1)}, u32[]{:S(2)}) copy-start(f32[4096,256]{1,0:T(8,128)S(1)} %fusion.49) | copy-start | bytes 12582916
  380.8 7.3 %copy-start.21 = (s32[1,32]{1,0:T(1,128)S(1)}, s32[1,32]{1,0:T(1,128)}, u32[]{:S(2)}) copy-start(s32[1,32]{1,0:T(1,128)} %param.15) | copy-start | bytes 388
  393.0 177.3 %reduce-scatter.2.cloned.1.call-start = ((), (), s32[]{:S(2)}) async-start(), calls=%async_computation.3 | async-start | bytes 1310720 | tf_op jit(solution)/shard_map/reduce_scatter | solution.py:111
  478.0 65.8 %copy-start.18 = (f32[256,256]{1,0:T(8,128)}, f32[256,256]{1,0:T(8,128)S(1)}, u32[]{:S(2)}) copy-start(f32[256,256]{1,0:T(8,128)S(1)} %fusion.47) | copy-start | bytes 786436
  490.0 53.9 %copy-start.20 = (s32[1,8]{1,0:T(1,128)S(1)}, s32[1,8]{1,0:T(1,128)}, u32[]{:S(2)}) copy-start(s32[1,8]{1,0:T(1,128)} %param.16) | copy-start | bytes 100
Sparse Core Ops, SparseCore 0:
  71.4 74.3 all-reduce.5
  239.6 72.3 all-reduce.7
  393.1 83.0 all-reduce.9
  546.2 24.0 reduce-scatter.1
where the time goes:
time: 581 us; the launch traced here: 577 us
  waiting for transfers between devices  215 us (37%)
  other arithmetic  178 us (31%)
  matrix products  123 us (21%)
  local copies, waits for them, and re-layouts  22.2 us (4%)
  starting transfers between devices  18.6 us (3%)
  between operations  18.6 us (3%)
    psum x3, waiting for transfers between devices, local(): lax.psum((gram_matrix(filtered, mass_part), gram_matrix(filtered, stiff_p...  191 us
    another operation x20, other arithmetic, lower_inverse(): factor = jnp.linalg.cholesky(matrix)  103 us
    another operation x7, other arithmetic, lower_inverse(): lax.linalg.triangular_solve(factor, unit_matrix, left_side=True, lower=True)  59.6 us
    dot_general x8, matrix products, block_product(): return jnp.einsum('bij,bjm->bim', blocks, vectors, precision=highest)  43.4 us
    reduce_scatter x1, waiting for transfers between devices, local(): owned = lax.psum_scatter(dense_sum, 'comp', scatter_dimension=0, tiled=True)  24.2 us
    dot_general x3, matrix products, gram_matrix(): return jnp.dot(left.T, right, precision=highest) / dof_count  22.8 us
    dot_general x3, matrix products, stiff_apply(): jnp.einsum('bji,bjm->bim', link_after, extended[2:], precision=highest)  19.3 us
    ppermute x3, starting transfers between devices, extended_2(): lax.ppermute(lax.slice_in_dim(block, block.shape[dim] - width, None, axis...  12.7 us
  transfers between devices with their start and end apart: 11, of which 4 were waited for; matrix products, arithmetic and copies ran while one was open for 13% of the time, Pallas kernels for 0%

commit v1 on v0

--- a/solution.py
+++ b/solution.py
@@ -34,12 +34,6 @@
     return jnp.einsum("bij,bjm->bim", blocks, vectors, precision=highest)
 
 
-def lower_inverse(matrix):
-    factor = jnp.linalg.cholesky(matrix)
-    unit_matrix = jnp.eye(matrix.shape[0], dtype=matrix.dtype)
-    return lax.linalg.triangular_solve(factor, unit_matrix, left_side=True, lower=True)
-
-
 def local(start_modes, stiff_diag, stiff_off, mass_blocks, coupling, interface_block, global_iface):
     start_flat = start_modes[0]
     stiff_self = stiff_diag[0]
@@ -64,44 +58,51 @@
         result = result + jnp.einsum("bji,bjm->bim", link_after, extended[2:], precision=highest)
         return result.reshape(row_count, mode_count)
 
+    def mass_apply(vectors):
+        return block_product(
+            mass_self, vectors.reshape(blocks_dev, block_size, mode_count)
+        ).reshape(row_count, mode_count)
+
     def gram_matrix(left, right):
-        return jnp.dot(left.T, right, precision=highest) / dof_count
+        return jnp.dot(left.T, right, precision=highest)
 
-    basis = start_flat
-    stiff_basis = stiff_apply(basis)
-    reduced = jnp.zeros((mode_count, mode_count), jnp.float32)
-    for sweep in range(ITERS):
-        filtered = basis - step_size * stiff_basis
-        mass_part = block_product(
-            mass_self, filtered.reshape(blocks_dev, block_size, mode_count)
-        ).reshape(row_count, mode_count)
-        stiff_part = stiff_apply(filtered)
-        mass_gram, stiff_gram = lax.psum(
-            (gram_matrix(filtered, mass_part), gram_matrix(filtered, stiff_part)), "blk"
-        )
-        factor_inv = lower_inverse(mass_gram)
-        basis = jnp.dot(filtered, factor_inv.T, precision=highest)
-        if sweep + 1 < ITERS:
-            stiff_basis = jnp.dot(stiff_part, factor_inv.T, precision=highest)
-        reduced = jnp.dot(
-            jnp.dot(factor_inv, stiff_gram, precision=highest), factor_inv.T, precision=highest
-        )
+    first = start_flat - step_size * stiff_apply(start_flat)
+    second = first - step_size * stiff_apply(first)
+    stiff_second = stiff_apply(second)
     iface_count = global_ids.shape[0]
     block_terms = jnp.einsum(
         "bkm,bkl->bml",
-        basis.reshape(blocks_dev, block_size, mode_count),
+        second.reshape(blocks_dev, block_size, mode_count),
         coupling_blocks,
         precision=highest,
     )
     onehot = (interface_ids[:, None] == jnp.arange(iface_count, dtype=jnp.int32)[None, :]).astype(
         jnp.float32
     )
-    coupling_term = (
-        jnp.einsum("bj,bml->mjl", onehot, block_terms, precision=highest) / dof_count**0.5
+    coupling_term = jnp.einsum("bj,bml->mjl", onehot, block_terms, precision=highest)
+    first_gram, mass_gram, stiff_gram, coupling_sum = lax.psum(
+        (
+            gram_matrix(first, mass_apply(first)),
+            gram_matrix(second, mass_apply(second)),
+            gram_matrix(second, stiff_second),
+            coupling_term,
+        ),
+        "blk",
     )
-    reduced_inv = lower_inverse(reduced)
-    shared = lax.psum(coupling_term, "blk")
-    scaled = jnp.einsum("nm,mjl->njl", reduced_inv, shared, precision=highest)
+    factors = jnp.linalg.cholesky(jnp.stack([first_gram, mass_gram, stiff_gram]) / dof_count)
+    guard = 0.0 * jnp.sum(factors[0])
+    unit_matrix = jnp.broadcast_to(jnp.eye(mode_count, dtype=jnp.float32), (2, mode_count, mode_count))
+    inverses = lax.linalg.triangular_solve(factors[1:], unit_matrix, left_side=True, lower=True)
+    factor_inv = inverses[0] + guard
+    chain_inv = inverses[1] + guard
+    basis = jnp.dot(second, factor_inv.T, precision=highest)
+    reduced = (
+        jnp.dot(
+            jnp.dot(factor_inv, stiff_gram, precision=highest), factor_inv.T, precision=highest
+        )
+        / dof_count
+    )
+    scaled = jnp.einsum("nm,mjl->njl", chain_inv, coupling_sum, precision=highest) / dof_count**0.5
     condensed = jnp.einsum("njk,njl->jkl", scaled, scaled, precision=highest)
     global_count = GIFC * lax.axis_size("comp")
     placed = (global_ids[:, None] == jnp.arange(global_count, dtype=jnp.int32)[None, :]).astype(

time: 581 us -> 466 us (0.80)
  waiting for transfers between devices: 215 us -> 116 us
  other arithmetic: 178 us -> 166 us
  local copies, waits for them, and re-layouts: 22.2 us -> 13.2 us
  matrix products: 123 us -> 130 us
    psum x3 -> x1, waiting for transfers between devices: 191 us -> 101 us  [local(): lax.psum((gram_matrix(first, mass_apply(first)), gram_matrix(second, mass...]
    another operation x27 -> x13, other arithmetic: 163 us -> 140 us  [the longest x9 101 us: local(): jnp.linalg.cholesky(jnp.stack([first_gram, mass_gram, stiff_gram]) / dof_...]
    reduce_scatter x1, waiting for transfers between devices: 24.2 us -> 15.5 us  [local(): owned = lax.psum_scatter(dense_sum, 'comp', scatter_dimension=0, tiled=True)]
    sub x2 -> x3, other arithmetic: 1.35 us -> 9.83 us  [the longest x2 7.1 us: local(): second = first - step_size * stiff_apply(first)]
    another operation x28 -> x10, local copies, waits for them, and re-layouts: 11.7 us -> 4.06 us  [the longest x22 11.6 us: lower_inverse(): lax.linalg.triangular_solve(factor, unit_matrix, left_side=True, lower=True)]
    dot_general x8, matrix products: 43.4 us -> 49.9 us  [block_product(): return jnp.einsum('bij,bjm->bim', blocks, vectors, precision=highest)]
    dot_general x8 -> x6, matrix products: 47.3 us -> 47.1 us  [the longest x3 27.7 us: gram_matrix(): return jnp.dot(left.T, right, precision=highest)]
  transfers between devices with their start and end apart: 11 -> 9, of which waited for: 4 -> 2; matrix products, arithmetic and copies ran while one was open for 13% -> 18% of each run, Pallas kernels for 0% -> 0%
where the time goes in v1:
time: 466 us; the launch traced here: 462 us
  other arithmetic  166 us (36%)
  matrix products  130 us (28%)
  waiting for transfers between devices  116 us (25%)
  starting transfers between devices  20.8 us (4%)
  between operations  15.4 us (3%)
  local copies, waits for them, and re-layouts  13.2 us (3%)
    psum x1, waiting for transfers between devices, local(): lax.psum((gram_matrix(first, mass_apply(first)), gram_matrix(second, mass...  101 us
    another operation x9, other arithmetic, local(): jnp.linalg.cholesky(jnp.stack([first_gram, mass_gram, stiff_gram]) / dof_...  101 us
    dot_general x8, matrix products, block_product(): return jnp.einsum('bij,bjm->bim', blocks, vectors, precision=highest)  49.9 us
    another operation x4, other arithmetic, local(): lax.linalg.triangular_solve(factors[1:], unit_matrix, left_side=True, low...  39.6 us
    dot_general x3, matrix products, gram_matrix(): return jnp.dot(left.T, right, precision=highest)  27.7 us
    dot_general x3, matrix products, stiff_apply(): jnp.einsum('bji,bjm->bim', link_after, extended[2:], precision=highest)  21.5 us
    ppermute x3, starting transfers between devices, extended_2(): lax.ppermute(lax.slice_in_dim(block, block.shape[dim] - width, None, axis...  15.5 us
    reduce_scatter x1, waiting for transfers between devices, local(): owned = lax.psum_scatter(dense_sum, 'comp', scatter_dimension=0, tiled=True)  15.5 us
  transfers between devices with their start and end apart: 9, of which 2 were waited for; matrix products, arithmetic and copies ran while one was open for 18% of the time, Pallas kernels for 0%

profile of v1, /device:TPU:0, one launch (start us, length us, event | category | flops | bytes accessed | tf_op | source)
XLA Modules:
  0.0 461.6 jit_solution(6677137671491948520)
XLA Ops:
  7.2 1.1 slice_bitcast_fusion.4
  8.4 4.9 %collective-permute-start = (f32[128,256]{1,0:T(8,128)S(1)}, f32[128,256]{1,0:T(8,128)S(1)}, u32[]{:S(2)}, u32[]{:S(2)}) collective-permute-start(f32[128,256]{1,0:T(8,128)S(1)} %get-tuple-element.43), channel_id=1, source_target_pairs={{0,1},{1,2},{2,3},{3,4},{4,5},{5,6},{6,7},{8,9},{9,10},{10,11},{11... | collective-permute-start | bytes 393224 | tf_op jit(solution)/shard_map/ppermute | solution.py:25
  13.2 1.3 collective-permute-start.2
  16.1 1.3 collective-permute-start.1
  17.4 8.2 %fusion.28 = f32[32,128,256]{2,1,0:T(8,128)} fusion(f32[32,128,256]{2,1,0:T(8,128)} %bitcast.161, f32[1,32,128,128]{3,2,1,0:T(8,128)S(1)} %copy-done), kind=kOutput, calls=%fused_computation.45 | convolution fusion | flops 1610612736 | bytes 10485760 | tf_op jit(solution)/shard_map/bij,bjm->bim/dot_general | solution.py:34
  25.6 1.5 slice.147
  27.1 3.2 copy.61
  30.3 4.1 pad_maximum_fusion.4
  34.4 5.3 %fusion.22 = f32[32,256,128]{1,2,0:T(8,128)} fusion(f32[32,128,256]{2,1,0:T(8,128)S(1)} %bitcast.170, f32[1,32,128,128]{3,2,1,0:T(8,128)S(1)} %copy-done.7), kind=kOutput, calls=%fused_computation.39 | convolution fusion | flops 1610612736 | bytes 10485760 | tf_op jit(solution)/shard_map/bij,bjm->bim/dot_general | solution.py:34
  39.7 10.5 %fusion.77 = (f32[32,128,256]{2,1,0:T(8,128)S(1)}, f32[32,128,256]{2,1,0:T(8,128)}) fusion(f32[32,128,256]{2,1,0:T(8,128)S(1)} %bitcast.163, f32[32,128,256]{2,1,0:T(8,128)S(1)} %bitcast.173, f32[1,128,128]{1,2,0:T(8,128)} %collective-permute-done.1, f32[31,128,128]{1,2,0:T(8,128)S(1)} %bitcast.165, f32[32,128,256]{2,1,0:T(8,128)} %fusion.28, ...), kind=kOutput, calls=%fused_computation.115 | convolution fusion | flops 1615331328 | bytes 27262976 | tf_op jit(solution)/shard_map/bji,bjm->bim/dot_general | solution.py:58
  50.1 2.7 bitcast_subtract_fusion.2
  52.9 5.8 %collective-permute-start.3 = (f32[128,256]{1,0:T(8,128)S(1)}, f32[128,256]{1,0:T(8,128)}, u32[]{:S(2)}, u32[]{:S(2)}) collective-permute-start(f32[128,256]{1,0:T(8,128)S(1)} %get-tuple-element.39), channel_id=1, source_target_pairs={{0,1},{1,2},{2,3},{3,4},{4,5},{5,6},{6,7},{8,9},{9,10},{10,11},{11... | collective-permute-start | bytes 393224 | tf_op jit(solution)/shard_map/ppermute | solution.py:25
  58.7 1.3 collective-permute-start.4
  60.0 5.8 %fusion.26 = f32[32,256,128]{1,2,0:T(8,128)} fusion(f32[32,128,256]{2,1,0:T(8,128)S(1)} %get-tuple-element.47, f32[1,32,128,128]{3,2,1,0:T(8,128)S(1)} %copy-done), kind=kOutput, calls=%fused_computation.43 | convolution fusion | flops 1610612736 | bytes 10485760 | tf_op jit(solution)/shard_map/bij,bjm->bim/dot_general | solution.py:34
  65.9 5.5 %fusion.16 = f32[32,256,128]{1,2,0:T(8,128)} fusion(f32[32,128,256]{2,1,0:T(8,128)S(1)} %get-tuple-element.47, f32[1,32,128,128]{3,2,1,0:T(8,128)S(1)} %copy-done.17), kind=kOutput, calls=%fused_computation.33 | convolution fusion | flops 1610612736 | bytes 10485760 | tf_op jit(solution)/shard_map/bij,bjm->bim/dot_general | solution.py:34
  71.4 4.9 %pad_maximum_fusion.2 = (f32[4096,256]{1,0:T(8,128)}, f32[4096,256]{1,0:T(8,128)}) fusion(f32[128,256]{1,0:T(8,128)} %collective-permute-done.4, f32[4096,256]{1,0:T(8,128)S(1)} %bitcast_subtract_fusion.2, f32[128,256]{1,0:T(8,128)} %collective-permute-done.3), kind=kLoop, calls=%fused_computation.5 | loop fusion | flops 2097152 | bytes 12845056 | tf_op jit(solution)/shard_map/concatenate | solution.py:29
  76.2 5.9 %fusion.20 = f32[32,256,128]{1,2,0:T(8,128)S(1)} fusion(f32[32,128,256]{2,1,0:T(8,128)} %bitcast.171, f32[1,32,128,128]{3,2,1,0:T(8,128)S(1)} %copy-done.7), kind=kOutput, calls=%fused_computation.37 | convolution fusion | flops 1610612736 | bytes 10485760 | tf_op jit(solution)/shard_map/bij,bjm->bim/dot_general | solution.py:34
  82.2 5.4 %fusion.7 = f32[32,128,256]{2,1,0:T(8,128)S(1)} fusion(f32[32,256,128]{1,2,0:T(8,128)S(1)} %copy-done.16, f32[32,256,128]{1,2,0:T(8,128)S(1)} %fusion.20, f32[32,128,256]{2,1,0:T(8,128)S(1)} %bitcast.175, f32[1,128,128]{1,2,0:T(8,128)} %collective-permute-done.1, f32[31,128,128]{1,2,0:T(8,128)S(1)} %bitcast.166), kind=kOutput, calls=%fused_computation.20 | convolution fusion | flops 1614282752 | bytes 18874368 | tf_op jit(solution)/shard_map/bji,bjm->bim/dot_general | solution.py:58
  87.6 7.8 %fusion.14 = f32[32,256,128]{1,2,0:T(8,128)} fusion(f32[1,32,128,128]{3,2,1,0:T(8,128)} %param.10, f32[32,128,256]{2,1,0:T(8,128)S(1)} %get-tuple-element.47, f32[32,128,256]{2,1,0:T(8,128)S(1)} %fusion.7), kind=kOutput, calls=%fused_computation.31 | convolution fusion | flops 1611661312 | bytes 14680064 | tf_op jit(solution)/shard_map/bij,bjm->bim/dot_general | solution.py:34
  96.2 5.5 %fusion.24 = f32[32,256,128]{1,2,0:T(8,128)} fusion(f32[1,32,128,128]{3,2,1,0:T(8,128)S(1)} %copy-done, f32[32,128,256]{2,1,0:T(8,128)S(1)} %get-tuple-element.47, f32[32,128,256]{2,1,0:T(8,128)S(1)} %fusion.7), kind=kOutput, calls=%fused_computation.41 | convolution fusion | flops 1611661312 | bytes 14680064 | tf_op jit(solution)/shard_map/bij,bjm->bim/dot_general | solution.py:34
  101.7 4.8 %collective-permute-start.5 = (f32[128,256]{1,0:T(8,128)S(1)}, f32[128,256]{1,0:T(8,128)S(1)}, u32[]{:S(2)}, u32[]{:S(2)}) collective-permute-start(f32[128,256]{1,0:T(8,128)S(1)} %get-tuple-element.35), channel_id=1, source_target_pairs={{0,1},{1,2},{2,3},{3,4},{4,5},{5,6},{6,7},{8,9},{9,10},{10,11},{11... | collective-permute-start | bytes 393224 | tf_op jit(solution)/shard_map/ppermute | solution.py:25
  106.5 1.3 collective-permute-start.6
  107.8 9.3 %fusion.12 = f32[32,256,128]{2,1,0:T(8,128)} fusion(f32[1,32,128,128]{3,2,1,0:T(8,128)S(1)} %copy-done.19, f32[32,128,256]{2,1,0:T(8,128)S(1)} %get-tuple-element.47, f32[32,128,256]{2,1,0:T(8,128)S(1)} %fusion.7), kind=kOutput, calls=%fused_computation.29 | convolution fusion | flops 1611661312 | bytes 14680064 | tf_op jit(solution)/shard_map/bkm,bkl->bml/dot_general | solution.py:73
  117.1 6.3 %bitcast_subtract_fusion.1 = (f32[1,4096,256]{2,1,0:T(8,128)S(1)}, f32[1,4096,256]{2,1,0:T(8,128)}) fusion(f32[1,4096,256]{2,1,0:T(8,128)} %param.7, f32[1,4096,256]{2,1,0:T(8,128)S(1)} %bitcast.160, f32[1,4096,256]{2,1,0:T(8,128)} %bitcast.164), kind=kLoop, calls=%fused_computation.18 | loop fusion | flops 2097152 | bytes 20971520 | tf_op jit(solution)/shard_map/sub | solution.py:70
  123.4 12.5 %fusion.36 = f32[1,256,256]{1,2,0:T(8,128)} fusion(f32[4096,256]{1,0:T(8,128)} %bitcast.172, f32[1,4096,256]{2,1,0:T(8,128)} %get-tuple-element.29), kind=kOutput, calls=%fused_computation.50 | convolution fusion | flops 3221225472 | bytes 8650752 | tf_op jit(solution)/shard_map/dot_general | solution.py:67
  135.9 7.6 %fusion.33 = f32[1,256,256]{1,2,0:T(8,128)} fusion(f32[4096,256]{1,0:T(8,128)S(1)} %bitcast.168, f32[1,4096,256]{2,1,0:T(8,128)S(1)} %get-tuple-element.28), kind=kOutput, calls=%fused_computation.49 | convolution fusion | flops 3221225472 | bytes 8650752 | tf_op jit(solution)/shard_map/dot_general | solution.py:67
  143.5 4.8 %fusion.30 = f32[256,8,128]{2,1,0:T(8,128)} fusion(f32[32,256,128]{2,1,0:T(8,128)S(1)} %copy-done.12, s32[32]{0:T(128)S(1)} %bitcast.180), kind=kOutput, calls=%fused_computation.47 | convolution fusion | flops 100663552 | bytes 5243008 | tf_op jit(solution)/shard_map/bj,bml->mjl/dot_general | solution.py:82
  148.3 4.1 pad_maximum_fusion
  152.4 6.0 %fusion.18 = f32[32,256,128]{1,2,0:T(8,128)S(1)} fusion(f32[32,128,256]{2,1,0:T(8,128)} %bitcast.169, f32[1,32,128,128]{3,2,1,0:T(8,128)S(1)} %copy-done.7), kind=kOutput, calls=%fused_computation.35 | convolution fusion | flops 1610612736 | bytes 10485760 | tf_op jit(solution)/shard_map/bij,bjm->bim/dot_general | solution.py:34
  158.4 5.7 %bitcast_add_fusion = f32[32,128,256]{2,1,0:T(8,128)S(1)} fusion(f32[32,256,128]{1,2,0:T(8,128)S(1)} %copy-done.13, f32[32,256,128]{1,2,0:T(8,128)S(1)} %fusion.18, f32[32,128,256]{2,1,0:T(8,128)S(1)} %bitcast.174, f32[1,128,128]{1,2,0:T(8,128)} %collective-permute-done.1, f32[31,128,128]{1,2,0:T(8,128)S(1)} %bitcast.167), kind=kOutput, calls=%fused_computation.9 | convolution fusion | flops 1613234176 | bytes 18874368 | tf_op jit(solution)/shard_map/bji,bjm->bim/dot_general | solution.py:58
  164.1 7.7 %fusion.3 = f32[256,256]{0,1:T(8,128)} fusion(f32[4096,256]{1,0:T(8,128)S(1)} %bitcast.176, f32[1,4096,256]{2,1,0:T(8,128)S(1)} %get-tuple-element.28), kind=kOutput, calls=%fused_computation.14 | convolution fusion | flops 3221225472 | bytes 8650752 | tf_op jit(solution)/shard_map/dot_general | solution.py:67
  172.0 100.9 %all-reduce.4.cloned.1.call-done = (f32[256,256]{0,1:T(8,128)}, f32[1,256,256]{1,2,0:T(8,128)}, f32[1,256,256]{1,2,0:T(8,128)}, f32[256,8,128]{2,1,0:T(8,128)}) async-done(((f32[256,256]{0,1:T(8,128)}, f32[1,256,256]{1,2,0:T(8,128)}, f32[1,256,256]{1,2,0:T(8,128)}, f32[256,8,128]{2,1,0:T(8,128)}), (f32[256,256]{0,1:T(8,128)}, f32[1,256,256]{1,2,0:T(8,128)}, f32[1,256,256]{1,2,0:T(8,128)}, ...) | async-done | bytes 1835024 | tf_op jit(solution)/shard_map/psum | solution.py:83
  272.9 1.2 maximum_multiply_fusion
  274.4 1.2 fusion.41
  275.6 35.6 %custom-call.16 = f32[3,128,128]{2,1,0:T(8,128)S(1)} custom-call(f32[3,128,128]{2,1,0:T(8,128)S(1)} %cholesky.122), custom_call_target="Cholesky" | custom-call | tf_op jit(solution)/shard_map/jit(cholesky)/cholesky | solution.py:92
  311.3 29.5 %custom-call.17 = f32[3,1,128,128]{2,3,1,0:T(8,128)S(1)} custom-call(f32[3,1,128,128]{3,2,1,0:T(8,128)S(1)} %select_bitcast_fusion), custom_call_target="InvertDiagBlocksLowerTriangular" | custom-call | tf_op jit(solution)/shard_map/jit(cholesky)/cholesky | solution.py:92
  341.7 35.2 %custom-call.18 = f32[3,128,128]{2,1,0:T(8,128)S(1)} custom-call(f32[3,128,128]{2,1,0:T(8,128)S(1)} %convolution_subtract_fusion.1), custom_call_target="Cholesky" | custom-call | tf_op jit(solution)/shard_map/jit(cholesky)/cholesky | solution.py:92
  378.0 3.9 while.1
  378.6 1.4 bitcast_dynamic-update-slice_fusion.2
  380.6 1.4 bitcast_dynamic-update-slice_fusion.2
  382.0 39.5 %custom-call.19 = f32[2,2,128,128]{2,3,1,0:T(8,128)S(1)} custom-call(f32[2,2,128,128]{3,2,1,0:T(8,128)S(1)} %bitcast.181), custom_call_target="InvertDiagBlocksLowerTriangular" | custom-call | tf_op jit(solution)/shard_map/triangular_solve | solution.py:95
  423.4 2.4 convolution_multiply_fusion
  425.8 1.9 fusion.79
  427.6 0.9 fusion.42
  428.5 1.3 copy.50
  430.3 1.1 fusion.39
  431.5 7.7 %convolution_bitcast_fusion = f32[1,4096,256]{2,1,0:T(8,128)} fusion(f32[256,256]{1,0:T(8,128)S(1)} %fusion.46, f32[1,4096,256]{2,1,0:T(8,128)} %copy-done.3), kind=kOutput, calls=%fused_computation.2 | convolution fusion | flops 3221225472 | bytes 8650752 | tf_op jit(solution)/shard_map/dot_general | solution.py:98
  439.1 15.5 %reduce-scatter.2.cloned.1.call-done = f32[4,128,128]{2,1,0:T(8,128)} async-done(((f32[16,128,128]{2,1,0:T(8,128)}), f32[4,128,128]{2,1,0:T(8,128)}) %reduce-scatter.2.cloned.1.call-update) | async-done | bytes 262160 | tf_op jit(solution)/shard_map/reduce_scatter | solution.py:112
  (89 shorter events, 8.0 us)
Async XLA Ops:
  7.2 10.2 %copy-start = (f32[1,32,128,128]{3,2,1,0:T(8,128)S(1)}, f32[1,32,128,128]{3,2,1,0:T(8,128)}, u32[]{:S(2)}) copy-start(f32[1,32,128,128]{3,2,1,0:T(8,128)} %param.8) | copy-start | bytes 6291460
  7.2 265.8 %all-reduce.4.cloned.1.call-start = ((), (), s32[]{:S(2)}) async-start(), calls=%async_computation.2 | async-start | bytes 3670016 | tf_op jit(solution)/shard_map/psum | solution.py:83
  8.4 21.9 %collective-permute-start = (f32[128,256]{1,0:T(8,128)S(1)}, f32[128,256]{1,0:T(8,128)S(1)}, u32[]{:S(2)}, u32[]{:S(2)}) collective-permute-start(f32[128,256]{1,0:T(8,128)S(1)} %get-tuple-element.43), channel_id=1, source_target_pairs={{0,1},{1,2},{2,3},{3,4},{4,5},{5,6},{6,7},{8,9},{9,10},{10,11},{11... | collective-permute-start | bytes 393224 | tf_op jit(solution)/shard_map/ppermute | solution.py:25
  13.2 17.0 %collective-permute-start.2 = (f32[128,256]{1,0:T(8,128)S(1)}, f32[128,256]{1,0:T(8,128)S(1)}, u32[]{:S(2)}, u32[]{:S(2)}) collective-permute-start(f32[128,256]{1,0:T(8,128)S(1)} %get-tuple-element.42), channel_id=1, source_target_pairs={{1,0},{2,1},{3,2},{4,3},{5,4},{6,5},{7,6},{9,8},{10,9},{11,10},{12... | collective-permute-start | bytes 393224 | tf_op jit(solution)/shard_map/ppermute | solution.py:28
  16.1 23.5 %collective-permute-start.1 = (f32[1,128,128]{1,2,0:T(8,128)}, f32[1,128,128]{1,2,0:T(8,128)}, u32[]{:S(2)}, u32[]{:S(2)}) collective-permute-start(f32[1,128,128]{1,2,0:T(8,128)} %bitcast.8), channel_id=1, source_target_pairs={{1,0},{2,1},{3,2},{4,3},{5,4},{6,5},{7,6},{9,8},{10,9},{11,10},{12... | collective-permute-start | bytes 196616 | tf_op jit(solution)/shard_map/ppermute | solution.py:17
  17.4 8.2 %copy-start.6 = (f32[1,32,128,128]{3,2,1,0:T(8,128)S(1)}, f32[1,32,128,128]{3,2,1,0:T(8,128)}, u32[]{:S(2)}) copy-start(f32[1,32,128,128]{3,2,1,0:T(8,128)} %param.9) | copy-start | bytes 6291460
  30.3 4.1 copy-start.7
  34.4 5.3 %copy-start.2 = (f32[1,4096,256]{2,1,0:T(8,128)S(1)}, f32[1,4096,256]{2,1,0:T(8,128)}, u32[]{:S(2)}) copy-start(f32[1,4096,256]{2,1,0:T(8,128)} %param.7) | copy-start | bytes 12582916
  34.4 5.3 %copy-start.8 = (f32[1,31,128,128]{2,3,1,0:T(8,128)S(1)}, f32[1,31,128,128]{2,3,1,0:T(8,128)}, u32[]{:S(2)}) copy-start(f32[1,31,128,128]{2,3,1,0:T(8,128)} %copy.61) | copy-start | bytes 6094852
  52.9 18.5 %copy-start.4 = (f32[4096,256]{1,0:T(8,128)}, f32[4096,256]{1,0:T(8,128)S(1)}, u32[]{:S(2)}) copy-start(f32[4096,256]{1,0:T(8,128)S(1)} %bitcast_subtract_fusion.2) | copy-start | bytes 12582916
  52.9 18.4 %collective-permute-start.3 = (f32[128,256]{1,0:T(8,128)S(1)}, f32[128,256]{1,0:T(8,128)}, u32[]{:S(2)}, u32[]{:S(2)}) collective-permute-start(f32[128,256]{1,0:T(8,128)S(1)} %get-tuple-element.39), channel_id=1, source_target_pairs={{0,1},{1,2},{2,3},{3,4},{4,5},{5,6},{6,7},{8,9},{9,10},{10,11},{11... | collective-permute-start | bytes 393224 | tf_op jit(solution)/shard_map/ppermute | solution.py:25
  58.7 12.6 %collective-permute-start.4 = (f32[128,256]{1,0:T(8,128)S(1)}, f32[128,256]{1,0:T(8,128)}, u32[]{:S(2)}, u32[]{:S(2)}) collective-permute-start(f32[128,256]{1,0:T(8,128)S(1)} %get-tuple-element.38), channel_id=1, source_target_pairs={{1,0},{2,1},{3,2},{4,3},{5,4},{6,5},{7,6},{9,8},{10,9},{11,10},{12... | collective-permute-start | bytes 393224 | tf_op jit(solution)/shard_map/ppermute | solution.py:28
  60.0 5.9 %copy-start.17 = (f32[1,32,128,128]{3,2,1,0:T(8,128)S(1)}, f32[1,32,128,128]{3,2,1,0:T(8,128)}, u32[]{:S(2)}) copy-start(f32[1,32,128,128]{3,2,1,0:T(8,128)} %param.10) | copy-start | bytes 6291460
  76.2 5.9 %copy-start.15 = (f32[4096,256]{1,0:T(8,128)S(1)}, f32[4096,256]{1,0:T(8,128)}, u32[]{:S(2)}) copy-start(f32[4096,256]{1,0:T(8,128)} %get-tuple-element.36) | copy-start | bytes 12582916
  76.2 6.0 %copy-start.16 = (f32[32,256,128]{1,2,0:T(8,128)S(1)}, f32[32,256,128]{1,2,0:T(8,128)}, u32[]{:S(2)}) copy-start(f32[32,256,128]{1,2,0:T(8,128)} %fusion.26) | copy-start | bytes 12582916
  87.6 7.8 %copy-start.5 = (f32[4096,256]{1,0:T(8,128)S(1)}, f32[4096,256]{1,0:T(8,128)}, u32[]{:S(2)}) copy-start(f32[4096,256]{1,0:T(8,128)} %copy-done.4) | copy-start | bytes 12582916
  96.2 5.5 %copy-start.9 = (f32[4096,256]{1,0:T(8,128)}, f32[4096,256]{1,0:T(8,128)S(1)}, u32[]{:S(2)}) copy-start(f32[4096,256]{1,0:T(8,128)S(1)} %bitcast_subtract_fusion) | copy-start | bytes 12582916
  96.2 11.6 %copy-start.19 = (f32[1,32,128,128]{3,2,1,0:T(8,128)S(1)}, f32[1,32,128,128]{3,2,1,0:T(8,128)}, u32[]{:S(2)}) copy-start(f32[1,32,128,128]{3,2,1,0:T(8,128)} %param.11) | copy-start | bytes 6291460
  101.7 46.6 %collective-permute-start.5 = (f32[128,256]{1,0:T(8,128)S(1)}, f32[128,256]{1,0:T(8,128)S(1)}, u32[]{:S(2)}, u32[]{:S(2)}) collective-permute-start(f32[128,256]{1,0:T(8,128)S(1)} %get-tuple-element.35), channel_id=1, source_target_pairs={{0,1},{1,2},{2,3},{3,4},{4,5},{5,6},{6,7},{8,9},{9,10},{10,11},{11... | collective-permute-start | bytes 393224 | tf_op jit(solution)/shard_map/ppermute | solution.py:25
  106.5 41.8 %collective-permute-start.6 = (f32[128,256]{1,0:T(8,128)S(1)}, f32[128,256]{1,0:T(8,128)S(1)}, u32[]{:S(2)}, u32[]{:S(2)}) collective-permute-start(f32[128,256]{1,0:T(8,128)S(1)} %get-tuple-element.34), channel_id=1, source_target_pairs={{1,0},{2,1},{3,2},{4,3},{5,4},{6,5},{7,6},{9,8},{10,9},{11,10},{12... | collective-permute-start | bytes 393224 | tf_op jit(solution)/shard_map/ppermute | solution.py:28
  123.4 40.7 %copy-start.3 = (f32[1,4096,256]{2,1,0:T(8,128)}, f32[1,4096,256]{2,1,0:T(8,128)S(1)}, u32[]{:S(2)}) copy-start(f32[1,4096,256]{2,1,0:T(8,128)S(1)} %get-tuple-element.28) | copy-start | bytes 12582916
  123.4 12.5 %copy-start.11 = (f32[32,256,128]{1,2,0:T(8,128)S(1)}, f32[32,256,128]{1,2,0:T(8,128)}, u32[]{:S(2)}) copy-start(f32[32,256,128]{1,2,0:T(8,128)} %fusion.14) | copy-start | bytes 12582916
  135.9 7.6 %copy-start.12 = (f32[32,256,128]{2,1,0:T(8,128)S(1)}, f32[32,256,128]{2,1,0:T(8,128)}, u32[]{:S(2)}) copy-start(f32[32,256,128]{2,1,0:T(8,128)} %fusion.12) | copy-start | bytes 12582916
  135.9 7.6 %copy-start.21 = (s32[1,32]{1,0:T(1,128)S(1)}, s32[1,32]{1,0:T(1,128)}, u32[]{:S(2)}) copy-start(s32[1,32]{1,0:T(1,128)} %param.12) | copy-start | bytes 388
  143.5 4.8 %copy-start.10 = (f32[4096,256]{1,0:T(8,128)S(1)}, f32[4096,256]{1,0:T(8,128)}, u32[]{:S(2)}) copy-start(f32[4096,256]{1,0:T(8,128)} %copy-done.9) | copy-start | bytes 12582916
  152.4 6.0 %copy-start.13 = (f32[32,256,128]{1,2,0:T(8,128)S(1)}, f32[32,256,128]{1,2,0:T(8,128)}, u32[]{:S(2)}) copy-start(f32[32,256,128]{1,2,0:T(8,128)} %fusion.24) | copy-start | bytes 12582916
  152.4 6.0 %copy-start.14 = (f32[4096,256]{1,0:T(8,128)S(1)}, f32[4096,256]{1,0:T(8,128)}, u32[]{:S(2)}) copy-start(f32[4096,256]{1,0:T(8,128)} %get-tuple-element.32) | copy-start | bytes 12582916
  171.8 282.7 %reduce-scatter.2.cloned.1.call-start = ((), (), s32[]{:S(2)}) async-start(), calls=%async_computation.1 | async-start | bytes 1310720 | tf_op jit(solution)/shard_map/reduce_scatter | solution.py:112
  378.0 49.6 %copy-start.20 = (s32[1,8]{1,0:T(1,128)S(1)}, s32[1,8]{1,0:T(1,128)}, u32[]{:S(2)}) copy-start(s32[1,8]{1,0:T(1,128)} %param.13) | copy-start | bytes 100
  425.8 4.1 copy-start.18
  430.3 24.3 %copy-start.1 = (f32[1,32,128,128]{3,2,1,0:T(8,128)S(1)}, f32[1,32,128,128]{3,2,1,0:T(8,128)}, u32[]{:S(2)}) copy-start(f32[1,32,128,128]{3,2,1,0:T(8,128)} %param.8) | copy-start | bytes 6291460
Sparse Core Ops, SparseCore 0:
  172.0 100.9 all-reduce.3
  430.0 24.5 reduce-scatter.1

commit v2 on v1

--- a/solution.py
+++ b/solution.py
@@ -1,6 +1,8 @@
 import jax
 import jax.numpy as jnp
 from jax import lax
+from jax.experimental import pallas as pl
+from jax.experimental.pallas import tpu as pltpu
 from jax.sharding import PartitionSpec as P
 
 ITERS = 2
@@ -32,6 +34,61 @@
 
 def block_product(blocks, vectors):
     return jnp.einsum("bij,bjm->bim", blocks, vectors, precision=highest)
+
+
+def _inverse_factor_kernel(a_in, w_out, a_ref, x_ref):
+    batch, size, _ = a_in.shape
+    a_ref[...] = a_in[...]
+    rows = lax.broadcasted_iota(jnp.int32, (size, size), 0)
+    cols = lax.broadcasted_iota(jnp.int32, (size, size), 1)
+    eye = jnp.where(rows == cols, 1.0, 0.0).astype(jnp.float32)
+    x_ref[...] = jnp.broadcast_to(eye, (batch, size, size))
+    phase = 64
+    lanes = 128
+    sublanes = 8
+
+    def row_of(ref, k, col0, col1):
+        tile0 = pl.multiple_of((k // sublanes) * sublanes, sublanes)
+        tile = ref[:, pl.ds(tile0, sublanes), col0:col1]
+        sub = lax.broadcasted_iota(jnp.int32, tile.shape, 1) + tile0
+        return jnp.sum(jnp.where(sub == k, tile, 0.0), axis=1, keepdims=True)
+
+    for start in range(0, size, phase):
+        a_col0 = (start // lanes) * lanes
+        x_col1 = min(size, -(-(start + phase) // lanes) * lanes)
+
+        def step(k, carry, start=start, a_col0=a_col0, x_col1=x_col1):
+            row_a = row_of(a_ref, k, a_col0, size)
+            row_x = row_of(x_ref, k, 0, x_col1)
+            block0 = pl.multiple_of((k // lanes) * lanes, lanes)
+            col_block = a_ref[:, start:, pl.ds(block0, lanes)]
+            lane = lax.broadcasted_iota(jnp.int32, col_block.shape, 2) + block0
+            col = jnp.sum(jnp.where(lane == k, col_block, 0.0), axis=2, keepdims=True)
+            lane_a = lax.broadcasted_iota(jnp.int32, row_a.shape, 2) + a_col0
+            pivot = jnp.sum(jnp.where(lane_a == k, row_a, 0.0), axis=2, keepdims=True)
+            row_ids = lax.broadcasted_iota(jnp.int32, col.shape, 1) + start
+            mult = jnp.where(row_ids > k, col / pivot, 0.0)
+            a_ref[:, start:, a_col0:] = a_ref[:, start:, a_col0:] - mult * row_a
+            x_ref[:, start:, :x_col1] = x_ref[:, start:, :x_col1] - mult * row_x
+            return carry
+
+        lax.fori_loop(start, start + phase, step, 0)
+    pivots = jnp.sum(jnp.where(rows == cols, a_ref[...], 0.0), axis=2, keepdims=True)
+    w_out[...] = x_ref[...] * lax.rsqrt(pivots)
+
+
+def inverse_factors(matrices):
+    batch, size, _ = matrices.shape
+    return pl.pallas_call(
+        _inverse_factor_kernel,
+        out_shape=jax.ShapeDtypeStruct(matrices.shape, jnp.float32),
+        in_specs=[pl.BlockSpec(memory_space=pltpu.VMEM)],
+        out_specs=pl.BlockSpec(memory_space=pltpu.VMEM),
+        scratch_shapes=[
+            pltpu.VMEM(matrices.shape, jnp.float32),
+            pltpu.VMEM(matrices.shape, jnp.float32),
+        ],
+    )(matrices)
 
 
 def local(start_modes, stiff_diag, stiff_off, mass_blocks, coupling, interface_block, global_iface):
@@ -89,12 +146,11 @@
         ),
         "blk",
     )
-    factors = jnp.linalg.cholesky(jnp.stack([first_gram, mass_gram, stiff_gram]) / dof_count)
-    guard = 0.0 * jnp.sum(factors[0])
-    unit_matrix = jnp.broadcast_to(jnp.eye(mode_count, dtype=jnp.float32), (2, mode_count, mode_count))
-    inverses = lax.linalg.triangular_solve(factors[1:], unit_matrix, left_side=True, lower=True)
-    factor_inv = inverses[0] + guard
-    chain_inv = inverses[1] + guard
+    grams = jnp.stack([first_gram, mass_gram, stiff_gram]) / dof_count
+    inverses = inverse_factors(0.5 * (grams + jnp.swapaxes(grams, 1, 2)))
+    guard = 0.0 * jnp.sum(inverses[0])
+    factor_inv = inverses[1] + guard
+    chain_inv = inverses[2] + guard
     basis = jnp.dot(second, factor_inv.T, precision=highest)
     reduced = (
         jnp.dot(

time: 466 us -> 372 us (0.80)
  other arithmetic: 166 us -> 27.8 us
  Pallas kernels: 0 us -> 51.2 us
    another operation x13 -> x0, other arithmetic: 140 us -> none  [the longest x9 101 us: local(): jnp.linalg.cholesky(jnp.stack([first_gram, mass_gram, stiff_gram]) / dof_...]
    pallas_call x0 -> x1, Pallas kernels: none -> 51.2 us  [inverse_factors(): pl.pallas_call(_inverse_factor_kernel, out_shape=jax.ShapeDtypeStruct(mat...]
  transfers between devices with their start and end apart: 9 -> 9, of which waited for: 2 -> 2; matrix products, arithmetic and copies ran while one was open for 18% -> 20% of each run, Pallas kernels for 0% -> 0%
where the time goes in v2:
time: 372 us; the launch traced here: 368 us
  matrix products  127 us (34%)
  waiting for transfers between devices  117 us (31%)
  Pallas kernels  51.2 us (14%)
  other arithmetic  27.8 us (7%)
  starting transfers between devices  20.9 us (6%)
  between operations  15.3 us (4%)
  local copies, waits for them, and re-layouts  9.08 us (2%)
    psum x1, waiting for transfers between devices, local(): lax.psum((gram_matrix(first, mass_apply(first)), gram_matrix(second, mass...  101 us
    pallas_call x1, Pallas kernels, inverse_factors(): pl.pallas_call(_inverse_factor_kernel, out_shape=jax.ShapeDtypeStruct(mat...  51.2 us
    dot_general x8, matrix products, block_product(): return jnp.einsum('bij,bjm->bim', blocks, vectors, precision=highest)  50 us
    dot_general x3, matrix products, gram_matrix(): return jnp.dot(left.T, right, precision=highest)  27.8 us
    dot_general x3, matrix products, stiff_apply(): jnp.einsum('bji,bjm->bim', link_after, extended[2:], precision=highest)  21.5 us
    ppermute x3, starting transfers between devices, extended_2(): lax.ppermute(lax.slice_in_dim(block, block.shape[dim] - width, None, axis...  15.5 us
    reduce_scatter x1, waiting for transfers between devices, local(): owned = lax.psum_scatter(dense_sum, 'comp', scatter_dimension=0, tiled=True)  15.5 us
    concatenate x3, other arithmetic, extended_2(): block = jnp.concatenate([low, block, high], axis=dim)  13 us
  transfers between devices with their start and end apart: 9, of which 2 were waited for; matrix products, arithmetic and copies ran while one was open for 20% of the time, Pallas kernels for 0%

profile of v2, /device:TPU:0, one launch (start us, length us, event | category | flops | bytes accessed | tf_op | source)
XLA Modules:
  0.0 367.8 jit_solution(7863506542207298233)
XLA Ops:
  7.2 1.1 slice_bitcast_fusion
  8.4 4.9 %collective-permute-start = (f32[128,256]{1,0:T(8,128)S(1)}, f32[128,256]{1,0:T(8,128)S(1)}, u32[]{:S(2)}, u32[]{:S(2)}) collective-permute-start(f32[128,256]{1,0:T(8,128)S(1)} %get-tuple-element.23), channel_id=1, source_target_pairs={{0,1},{1,2},{2,3},{3,4},{4,5},{5,6},{6,7},{8,9},{9,10},{10,11},{11... | collective-permute-start | bytes 393224 | tf_op jit(solution)/shard_map/ppermute | solution.py:27
  13.2 1.3 collective-permute-start.2
  14.5 0.8 slice.102
  15.4 0.7 copy.42
  16.1 1.3 collective-permute-start.1
  17.4 8.1 %fusion.28 = f32[32,128,256]{2,1,0:T(8,128)} fusion(f32[32,128,256]{2,1,0:T(8,128)} %bitcast.129, f32[1,32,128,128]{3,2,1,0:T(8,128)S(1)} %copy-done), kind=kOutput, calls=%fused_computation.43 | convolution fusion | flops 1610612736 | bytes 10485760 | tf_op jit(solution)/shard_map/bij,bjm->bim/dot_general | solution.py:36
  25.6 1.5 slice.100
  27.1 3.1 copy.41
  30.2 4.1 %pad_maximum_fusion.4 = (f32[4096,256]{1,0:T(8,128)S(1)}, f32[4096,256]{1,0:T(8,128)S(1)}) fusion(f32[128,256]{1,0:T(8,128)S(1)} %collective-permute-done.2, f32[4096,256]{1,0:T(8,128)} %bitcast.130, f32[128,256]{1,0:T(8,128)S(1)} %collective-permute-done), kind=kLoop, calls=%fused_computation.5 | loop fusion | flops 2097152 | bytes 12845056 | tf_op jit(solution)/shard_map/concatenate | solution.py:31
  34.3 5.3 %fusion.22 = f32[32,256,128]{1,2,0:T(8,128)} fusion(f32[32,128,256]{2,1,0:T(8,128)S(1)} %bitcast.138, f32[1,32,128,128]{3,2,1,0:T(8,128)S(1)} %copy-done.7), kind=kOutput, calls=%fused_computation.37 | convolution fusion | flops 1610612736 | bytes 10485760 | tf_op jit(solution)/shard_map/bij,bjm->bim/dot_general | solution.py:36
  39.6 10.5 %fusion.69 = (f32[32,128,256]{2,1,0:T(8,128)S(1)}, f32[32,128,256]{2,1,0:T(8,128)}) fusion(f32[32,128,256]{2,1,0:T(8,128)S(1)} %bitcast.131, f32[32,128,256]{2,1,0:T(8,128)S(1)} %bitcast.141, f32[1,128,128]{1,2,0:T(8,128)} %collective-permute-done.1, f32[31,128,128]{1,2,0:T(8,128)S(1)} %bitcast.133, f32[32,128,256]{2,1,0:T(8,128)} %fusion.28, ...), kind=kOutput, calls=%fused_computation.83 | convolution fusion | flops 1615331328 | bytes 27262976 | tf_op jit(solution)/shard_map/bji,bjm->bim/dot_general | solution.py:115
  50.1 2.7 bitcast_subtract_fusion.2
  52.8 5.9 %collective-permute-start.3 = (f32[128,256]{1,0:T(8,128)S(1)}, f32[128,256]{1,0:T(8,128)}, u32[]{:S(2)}, u32[]{:S(2)}) collective-permute-start(f32[128,256]{1,0:T(8,128)S(1)} %get-tuple-element.19), channel_id=1, source_target_pairs={{0,1},{1,2},{2,3},{3,4},{4,5},{5,6},{6,7},{8,9},{9,10},{10,11},{11... | collective-permute-start | bytes 393224 | tf_op jit(solution)/shard_map/ppermute | solution.py:27
  58.7 1.3 collective-permute-start.4
  60.0 5.5 %fusion.26 = f32[32,256,128]{1,2,0:T(8,128)} fusion(f32[32,128,256]{2,1,0:T(8,128)S(1)} %get-tuple-element.24, f32[1,32,128,128]{3,2,1,0:T(8,128)S(1)} %copy-done), kind=kOutput, calls=%fused_computation.41 | convolution fusion | flops 1610612736 | bytes 10485760 | tf_op jit(solution)/shard_map/bij,bjm->bim/dot_general | solution.py:36
  65.5 5.5 %fusion.16 = f32[32,256,128]{1,2,0:T(8,128)} fusion(f32[32,128,256]{2,1,0:T(8,128)S(1)} %get-tuple-element.24, f32[1,32,128,128]{3,2,1,0:T(8,128)S(1)} %copy-done.17), kind=kOutput, calls=%fused_computation.31 | convolution fusion | flops 1610612736 | bytes 10485760 | tf_op jit(solution)/shard_map/bij,bjm->bim/dot_general | solution.py:36
  71.0 4.9 %pad_maximum_fusion.2 = (f32[4096,256]{1,0:T(8,128)}, f32[4096,256]{1,0:T(8,128)}) fusion(f32[128,256]{1,0:T(8,128)} %collective-permute-done.4, f32[4096,256]{1,0:T(8,128)S(1)} %bitcast_subtract_fusion.2, f32[128,256]{1,0:T(8,128)} %collective-permute-done.3), kind=kLoop, calls=%fused_computation.3 | loop fusion | flops 2097152 | bytes 12845056 | tf_op jit(solution)/shard_map/concatenate | solution.py:31
  75.9 6.2 %fusion.20 = f32[32,256,128]{1,2,0:T(8,128)S(1)} fusion(f32[32,128,256]{2,1,0:T(8,128)} %bitcast.139, f32[1,32,128,128]{3,2,1,0:T(8,128)S(1)} %copy-done.7), kind=kOutput, calls=%fused_computation.35 | convolution fusion | flops 1610612736 | bytes 10485760 | tf_op jit(solution)/shard_map/bij,bjm->bim/dot_general | solution.py:36
  82.1 5.4 %fusion.7 = f32[32,128,256]{2,1,0:T(8,128)S(1)} fusion(f32[32,256,128]{1,2,0:T(8,128)S(1)} %copy-done.16, f32[32,256,128]{1,2,0:T(8,128)S(1)} %fusion.20, f32[32,128,256]{2,1,0:T(8,128)S(1)} %bitcast.143, f32[1,128,128]{1,2,0:T(8,128)} %collective-permute-done.1, f32[31,128,128]{1,2,0:T(8,128)S(1)} %bitcast.134), kind=kOutput, calls=%fused_computation.18 | convolution fusion | flops 1614282752 | bytes 18874368 | tf_op jit(solution)/shard_map/bji,bjm->bim/dot_general | solution.py:115
  87.5 7.8 %fusion.14 = f32[32,256,128]{1,2,0:T(8,128)} fusion(f32[1,32,128,128]{3,2,1,0:T(8,128)} %param.10, f32[32,128,256]{2,1,0:T(8,128)S(1)} %get-tuple-element.24, f32[32,128,256]{2,1,0:T(8,128)S(1)} %fusion.7), kind=kOutput, calls=%fused_computation.29 | convolution fusion | flops 1611661312 | bytes 14680064 | tf_op jit(solution)/shard_map/bij,bjm->bim/dot_general | solution.py:36
  95.3 0.8 bitcast_subtract_fusion
  96.1 5.5 %fusion.24 = f32[32,256,128]{1,2,0:T(8,128)} fusion(f32[1,32,128,128]{3,2,1,0:T(8,128)S(1)} %copy-done, f32[32,128,256]{2,1,0:T(8,128)S(1)} %get-tuple-element.24, f32[32,128,256]{2,1,0:T(8,128)S(1)} %fusion.7), kind=kOutput, calls=%fused_computation.39 | convolution fusion | flops 1611661312 | bytes 14680064 | tf_op jit(solution)/shard_map/bij,bjm->bim/dot_general | solution.py:36
  101.6 8.9 %fusion.12 = f32[32,256,128]{2,1,0:T(8,128)} fusion(f32[1,32,128,128]{3,2,1,0:T(8,128)S(1)} %copy-done.20, f32[32,128,256]{2,1,0:T(8,128)S(1)} %get-tuple-element.24, f32[32,128,256]{2,1,0:T(8,128)S(1)} %fusion.7), kind=kOutput, calls=%fused_computation.27 | convolution fusion | flops 1611661312 | bytes 14680064 | tf_op jit(solution)/shard_map/bkm,bkl->bml/dot_general | solution.py:130
  110.5 4.8 %collective-permute-start.5 = (f32[128,256]{1,0:T(8,128)S(1)}, f32[128,256]{1,0:T(8,128)S(1)}, u32[]{:S(2)}, u32[]{:S(2)}) collective-permute-start(f32[128,256]{1,0:T(8,128)S(1)} %get-tuple-element.15), channel_id=1, source_target_pairs={{0,1},{1,2},{2,3},{3,4},{4,5},{5,6},{6,7},{8,9},{9,10},{10,11},{11... | collective-permute-start | bytes 393224 | tf_op jit(solution)/shard_map/ppermute | solution.py:27
  115.3 1.5 collective-permute-start.6
  116.8 6.3 %bitcast_subtract_fusion.1 = (f32[1,4096,256]{2,1,0:T(8,128)S(1)}, f32[1,4096,256]{2,1,0:T(8,128)}) fusion(f32[1,4096,256]{2,1,0:T(8,128)} %param.7, f32[1,4096,256]{2,1,0:T(8,128)S(1)} %bitcast.128, f32[1,4096,256]{2,1,0:T(8,128)} %bitcast.132), kind=kLoop, calls=%fused_computation.16 | loop fusion | flops 2097152 | bytes 20971520 | tf_op jit(solution)/shard_map/sub | solution.py:127
  123.0 12.5 %fusion.36 = f32[1,256,256]{1,2,0:T(8,128)} fusion(f32[4096,256]{1,0:T(8,128)} %bitcast.140, f32[1,4096,256]{2,1,0:T(8,128)} %get-tuple-element.11), kind=kOutput, calls=%fused_computation.48 | convolution fusion | flops 3221225472 | bytes 8650752 | tf_op jit(solution)/shard_map/dot_general | solution.py:124
  135.5 7.6 %fusion.33 = f32[1,256,256]{1,2,0:T(8,128)} fusion(f32[4096,256]{1,0:T(8,128)S(1)} %bitcast.136, f32[1,4096,256]{2,1,0:T(8,128)S(1)} %get-tuple-element.10), kind=kOutput, calls=%fused_computation.47 | convolution fusion | flops 3221225472 | bytes 8650752 | tf_op jit(solution)/shard_map/dot_general | solution.py:124
  143.2 4.8 %fusion.30 = f32[256,8,128]{2,1,0:T(8,128)} fusion(f32[32,256,128]{2,1,0:T(8,128)S(1)} %copy-done.12, s32[32]{0:T(128)S(1)} %bitcast.148), kind=kOutput, calls=%fused_computation.45 | convolution fusion | flops 100663552 | bytes 5243008 | tf_op jit(solution)/shard_map/bj,bml->mjl/dot_general | solution.py:139
  148.0 4.1 %pad_maximum_fusion = (f32[4096,256]{1,0:T(8,128)}, f32[4096,256]{1,0:T(8,128)}) fusion(f32[128,256]{1,0:T(8,128)S(1)} %collective-permute-done.6, f32[4096,256]{1,0:T(8,128)S(1)} %copy-done.10, f32[128,256]{1,0:T(8,128)S(1)} %collective-permute-done.5), kind=kLoop, calls=%fused_computation.1 | loop fusion | flops 2097152 | bytes 12845056 | tf_op jit(solution)/shard_map/concatenate | solution.py:31
  152.1 6.2 %fusion.18 = f32[32,256,128]{1,2,0:T(8,128)S(1)} fusion(f32[32,128,256]{2,1,0:T(8,128)} %bitcast.137, f32[1,32,128,128]{3,2,1,0:T(8,128)S(1)} %copy-done.7), kind=kOutput, calls=%fused_computation.33 | convolution fusion | flops 1610612736 | bytes 10485760 | tf_op jit(solution)/shard_map/bij,bjm->bim/dot_general | solution.py:36
  158.2 5.7 %bitcast_add_fusion = f32[32,128,256]{2,1,0:T(8,128)S(1)} fusion(f32[32,256,128]{1,2,0:T(8,128)S(1)} %copy-done.13, f32[32,256,128]{1,2,0:T(8,128)S(1)} %fusion.18, f32[32,128,256]{2,1,0:T(8,128)S(1)} %bitcast.142, f32[1,128,128]{1,2,0:T(8,128)} %collective-permute-done.1, f32[31,128,128]{1,2,0:T(8,128)S(1)} %bitcast.135), kind=kOutput, calls=%fused_computation.7 | convolution fusion | flops 1613234176 | bytes 18874368 | tf_op jit(solution)/shard_map/bji,bjm->bim/dot_general | solution.py:115
  163.9 7.7 %fusion.3 = f32[256,256]{0,1:T(8,128)} fusion(f32[4096,256]{1,0:T(8,128)S(1)} %bitcast.144, f32[1,4096,256]{2,1,0:T(8,128)S(1)} %get-tuple-element.10), kind=kOutput, calls=%fused_computation.12 | convolution fusion | flops 3221225472 | bytes 8650752 | tf_op jit(solution)/shard_map/dot_general | solution.py:124
  171.7 101.0 %all-reduce.3.cloned.1.call-done = (f32[256,256]{0,1:T(8,128)}, f32[1,256,256]{1,2,0:T(8,128)}, f32[1,256,256]{1,2,0:T(8,128)}, f32[256,8,128]{2,1,0:T(8,128)}) async-done(((f32[256,256]{0,1:T(8,128)}, f32[1,256,256]{1,2,0:T(8,128)}, f32[1,256,256]{1,2,0:T(8,128)}, f32[256,8,128]{2,1,0:T(8,128)}), (f32[256,256]{0,1:T(8,128)}, f32[1,256,256]{1,2,0:T(8,128)}, f32[1,256,256]{1,2,0:T(8,128)}, ...) | async-done | bytes 1835024 | tf_op jit(solution)/shard_map/psum | solution.py:140
  272.7 1.3 maximum_multiply_fusion
  274.0 0.3 copy.29
  274.3 2.1 fusion.41.a_in
  276.4 51.2 %shard_map.94 = f32[3,256,256]{2,1,0:T(8,128)} custom-call(f32[3,256,256]{2,1,0:T(8,128)} %fusion.41.a_in), custom_call_target="tpu_custom_call" | custom-call | tf_op jit(solution)/shard_map/pallas_call | solution.py:82
  327.6 1.6 slice_reduce_fusion
  329.9 2.1 convolution_multiply_fusion
  332.0 1.9 fusion.70
  333.9 0.9 fusion.42
  334.7 1.3 copy.35
  336.1 0.4 fusion.48
  336.6 1.1 fusion.39
  337.7 7.7 %convolution_bitcast_fusion = f32[1,4096,256]{2,1,0:T(8,128)} fusion(f32[1,4096,256]{2,1,0:T(8,128)} %copy-done.3, f32[3,256,256]{2,1,0:T(8,128)S(1)} %copy-done.18, f32[]{:T(128)S(6)} %mul.60), kind=kOutput, calls=%fused_computation | convolution fusion | flops 3221291008 | bytes 8650756 | tf_op jit(solution)/shard_map/dot_general | solution.py:154
  345.3 15.5 %reduce-scatter.2.cloned.1.call-done = f32[4,128,128]{2,1,0:T(8,128)} async-done(((f32[16,128,128]{2,1,0:T(8,128)}), f32[4,128,128]{2,1,0:T(8,128)}) %reduce-scatter.2.cloned.1.call-update) | async-done | bytes 262160 | tf_op jit(solution)/shard_map/reduce_scatter | solution.py:168
  (61 shorter events, 0.3 us)
Async XLA Ops:
  7.2 10.2 %copy-start = (f32[1,32,128,128]{3,2,1,0:T(8,128)S(1)}, f32[1,32,128,128]{3,2,1,0:T(8,128)}, u32[]{:S(2)}) copy-start(f32[1,32,128,128]{3,2,1,0:T(8,128)} %param.8) | copy-start | bytes 6291460
  7.2 265.6 %all-reduce.3.cloned.1.call-start = ((), (), s32[]{:S(2)}) async-start(), calls=%async_computation.2 | async-start | bytes 3670016 | tf_op jit(solution)/shard_map/psum | solution.py:140
  8.4 21.8 %collective-permute-start = (f32[128,256]{1,0:T(8,128)S(1)}, f32[128,256]{1,0:T(8,128)S(1)}, u32[]{:S(2)}, u32[]{:S(2)}) collective-permute-start(f32[128,256]{1,0:T(8,128)S(1)} %get-tuple-element.23), channel_id=1, source_target_pairs={{0,1},{1,2},{2,3},{3,4},{4,5},{5,6},{6,7},{8,9},{9,10},{10,11},{11... | collective-permute-start | bytes 393224 | tf_op jit(solution)/shard_map/ppermute | solution.py:27
  13.2 17.0 %collective-permute-start.2 = (f32[128,256]{1,0:T(8,128)S(1)}, f32[128,256]{1,0:T(8,128)S(1)}, u32[]{:S(2)}, u32[]{:S(2)}) collective-permute-start(f32[128,256]{1,0:T(8,128)S(1)} %get-tuple-element.22), channel_id=1, source_target_pairs={{1,0},{2,1},{3,2},{4,3},{5,4},{6,5},{7,6},{9,8},{10,9},{11,10},{12... | collective-permute-start | bytes 393224 | tf_op jit(solution)/shard_map/ppermute | solution.py:30
  16.1 23.5 %collective-permute-start.1 = (f32[1,128,128]{1,2,0:T(8,128)}, f32[1,128,128]{1,2,0:T(8,128)}, u32[]{:S(2)}, u32[]{:S(2)}) collective-permute-start(f32[1,128,128]{1,2,0:T(8,128)} %bitcast.8), channel_id=1, source_target_pairs={{1,0},{2,1},{3,2},{4,3},{5,4},{6,5},{7,6},{9,8},{10,9},{11,10},{12... | collective-permute-start | bytes 196616 | tf_op jit(solution)/shard_map/ppermute | solution.py:19
  17.4 8.2 %copy-start.6 = (f32[1,32,128,128]{3,2,1,0:T(8,128)S(1)}, f32[1,32,128,128]{3,2,1,0:T(8,128)}, u32[]{:S(2)}) copy-start(f32[1,32,128,128]{3,2,1,0:T(8,128)} %param.9) | copy-start | bytes 6291460
  30.2 4.1 %copy-start.7 = (f32[1,32,128,128]{3,2,1,0:T(8,128)S(1)}, f32[1,32,128,128]{3,2,1,0:T(8,128)}, u32[]{:S(2)}) copy-start(f32[1,32,128,128]{3,2,1,0:T(8,128)} %param.9) | copy-start | bytes 6291460
  34.3 5.3 %copy-start.2 = (f32[1,4096,256]{2,1,0:T(8,128)S(1)}, f32[1,4096,256]{2,1,0:T(8,128)}, u32[]{:S(2)}) copy-start(f32[1,4096,256]{2,1,0:T(8,128)} %param.7) | copy-start | bytes 12582916
  34.3 5.3 %copy-start.8 = (f32[1,31,128,128]{2,3,1,0:T(8,128)S(1)}, f32[1,31,128,128]{2,3,1,0:T(8,128)}, u32[]{:S(2)}) copy-start(f32[1,31,128,128]{2,3,1,0:T(8,128)} %copy.41) | copy-start | bytes 6094852
  52.8 18.2 %copy-start.4 = (f32[4096,256]{1,0:T(8,128)}, f32[4096,256]{1,0:T(8,128)S(1)}, u32[]{:S(2)}) copy-start(f32[4096,256]{1,0:T(8,128)S(1)} %bitcast_subtract_fusion.2) | copy-start | bytes 12582916
  52.8 18.2 %collective-permute-start.3 = (f32[128,256]{1,0:T(8,128)S(1)}, f32[128,256]{1,0:T(8,128)}, u32[]{:S(2)}, u32[]{:S(2)}) collective-permute-start(f32[128,256]{1,0:T(8,128)S(1)} %get-tuple-element.19), channel_id=1, source_target_pairs={{0,1},{1,2},{2,3},{3,4},{4,5},{5,6},{6,7},{8,9},{9,10},{10,11},{11... | collective-permute-start | bytes 393224 | tf_op jit(solution)/shard_map/ppermute | solution.py:27
  58.7 12.3 %collective-permute-start.4 = (f32[128,256]{1,0:T(8,128)S(1)}, f32[128,256]{1,0:T(8,128)}, u32[]{:S(2)}, u32[]{:S(2)}) collective-permute-start(f32[128,256]{1,0:T(8,128)S(1)} %get-tuple-element.18), channel_id=1, source_target_pairs={{1,0},{2,1},{3,2},{4,3},{5,4},{6,5},{7,6},{9,8},{10,9},{11,10},{12... | collective-permute-start | bytes 393224 | tf_op jit(solution)/shard_map/ppermute | solution.py:30
  60.0 5.5 %copy-start.17 = (f32[1,32,128,128]{3,2,1,0:T(8,128)S(1)}, f32[1,32,128,128]{3,2,1,0:T(8,128)}, u32[]{:S(2)}) copy-start(f32[1,32,128,128]{3,2,1,0:T(8,128)} %param.10) | copy-start | bytes 6291460
  75.9 6.2 %copy-start.15 = (f32[4096,256]{1,0:T(8,128)S(1)}, f32[4096,256]{1,0:T(8,128)}, u32[]{:S(2)}) copy-start(f32[4096,256]{1,0:T(8,128)} %get-tuple-element.16) | copy-start | bytes 12582916
  75.9 6.2 %copy-start.16 = (f32[32,256,128]{1,2,0:T(8,128)S(1)}, f32[32,256,128]{1,2,0:T(8,128)}, u32[]{:S(2)}) copy-start(f32[32,256,128]{1,2,0:T(8,128)} %fusion.26) | copy-start | bytes 12582916
  87.5 7.8 %copy-start.5 = (f32[4096,256]{1,0:T(8,128)S(1)}, f32[4096,256]{1,0:T(8,128)}, u32[]{:S(2)}) copy-start(f32[4096,256]{1,0:T(8,128)} %copy-done.4) | copy-start | bytes 12582916
  96.1 14.4 %copy-start.9 = (f32[4096,256]{1,0:T(8,128)}, f32[4096,256]{1,0:T(8,128)S(1)}, u32[]{:S(2)}) copy-start(f32[4096,256]{1,0:T(8,128)S(1)} %bitcast_subtract_fusion) | copy-start | bytes 12582916
  96.1 5.5 %copy-start.20 = (f32[1,32,128,128]{3,2,1,0:T(8,128)S(1)}, f32[1,32,128,128]{3,2,1,0:T(8,128)}, u32[]{:S(2)}) copy-start(f32[1,32,128,128]{3,2,1,0:T(8,128)} %param.11) | copy-start | bytes 6291460
  110.5 37.5 %collective-permute-start.5 = (f32[128,256]{1,0:T(8,128)S(1)}, f32[128,256]{1,0:T(8,128)S(1)}, u32[]{:S(2)}, u32[]{:S(2)}) collective-permute-start(f32[128,256]{1,0:T(8,128)S(1)} %get-tuple-element.15), channel_id=1, source_target_pairs={{0,1},{1,2},{2,3},{3,4},{4,5},{5,6},{6,7},{8,9},{9,10},{10,11},{11... | collective-permute-start | bytes 393224 | tf_op jit(solution)/shard_map/ppermute | solution.py:27
  115.3 32.7 %collective-permute-start.6 = (f32[128,256]{1,0:T(8,128)S(1)}, f32[128,256]{1,0:T(8,128)S(1)}, u32[]{:S(2)}, u32[]{:S(2)}) collective-permute-start(f32[128,256]{1,0:T(8,128)S(1)} %get-tuple-element.14), channel_id=1, source_target_pairs={{1,0},{2,1},{3,2},{4,3},{5,4},{6,5},{7,6},{9,8},{10,9},{11,10},{12... | collective-permute-start | bytes 393224 | tf_op jit(solution)/shard_map/ppermute | solution.py:30
  123.0 40.9 %copy-start.3 = (f32[1,4096,256]{2,1,0:T(8,128)}, f32[1,4096,256]{2,1,0:T(8,128)S(1)}, u32[]{:S(2)}) copy-start(f32[1,4096,256]{2,1,0:T(8,128)S(1)} %get-tuple-element.10) | copy-start | bytes 12582916
  123.0 12.5 %copy-start.11 = (f32[32,256,128]{1,2,0:T(8,128)S(1)}, f32[32,256,128]{1,2,0:T(8,128)}, u32[]{:S(2)}) copy-start(f32[32,256,128]{1,2,0:T(8,128)} %fusion.14) | copy-start | bytes 12582916
  135.5 7.6 %copy-start.12 = (f32[32,256,128]{2,1,0:T(8,128)S(1)}, f32[32,256,128]{2,1,0:T(8,128)}, u32[]{:S(2)}) copy-start(f32[32,256,128]{2,1,0:T(8,128)} %fusion.12) | copy-start | bytes 12582916
  135.5 7.6 %copy-start.23 = (s32[1,32]{1,0:T(1,128)S(1)}, s32[1,32]{1,0:T(1,128)}, u32[]{:S(2)}) copy-start(s32[1,32]{1,0:T(1,128)} %param.12) | copy-start | bytes 388
  143.2 4.8 %copy-start.10 = (f32[4096,256]{1,0:T(8,128)S(1)}, f32[4096,256]{1,0:T(8,128)}, u32[]{:S(2)}) copy-start(f32[4096,256]{1,0:T(8,128)} %copy-done.9) | copy-start | bytes 12582916
  152.1 6.2 %copy-start.13 = (f32[32,256,128]{1,2,0:T(8,128)S(1)}, f32[32,256,128]{1,2,0:T(8,128)}, u32[]{:S(2)}) copy-start(f32[32,256,128]{1,2,0:T(8,128)} %fusion.24) | copy-start | bytes 12582916
  152.1 6.2 %copy-start.14 = (f32[4096,256]{1,0:T(8,128)S(1)}, f32[4096,256]{1,0:T(8,128)}, u32[]{:S(2)}) copy-start(f32[4096,256]{1,0:T(8,128)} %get-tuple-element.12) | copy-start | bytes 12582916
  171.7 189.1 %reduce-scatter.2.cloned.1.call-start = ((), (), s32[]{:S(2)}) async-start(), calls=%async_computation.1 | async-start | bytes 1310720 | tf_op jit(solution)/shard_map/reduce_scatter | solution.py:168
  272.7 57.1 %copy-start.21 = (f32[256,8,128]{2,1,0:T(8,128)S(1)}, f32[256,8,128]{2,1,0:T(8,128)}, u32[]{:S(2)}) copy-start(f32[256,8,128]{2,1,0:T(8,128)} %get-tuple-element.9) | copy-start | bytes 3145732
  274.3 59.6 %copy-start.22 = (s32[1,8]{1,0:T(1,128)S(1)}, s32[1,8]{1,0:T(1,128)}, u32[]{:S(2)}) copy-start(s32[1,8]{1,0:T(1,128)} %param.13) | copy-start | bytes 100
  332.0 4.1 %copy-start.18 = (f32[3,256,256]{2,1,0:T(8,128)S(1)}, f32[3,256,256]{2,1,0:T(8,128)}, u32[]{:S(2)}) copy-start(f32[3,256,256]{2,1,0:T(8,128)} %shard_map.94) | copy-start | bytes 2359300
  332.0 4.1 %copy-start.19 = (f32[256,256]{0,1:T(8,128)S(1)}, f32[256,256]{0,1:T(8,128)}, u32[]{:S(2)}) copy-start(f32[256,256]{0,1:T(8,128)} %get-tuple-element.6) | copy-start | bytes 786436
  336.5 24.3 %copy-start.1 = (f32[1,32,128,128]{3,2,1,0:T(8,128)S(1)}, f32[1,32,128,128]{3,2,1,0:T(8,128)}, u32[]{:S(2)}) copy-start(f32[1,32,128,128]{3,2,1,0:T(8,128)} %param.8) | copy-start | bytes 6291460
Sparse Core Ops, SparseCore 0:
  171.8 100.8 all-reduce.2
  336.2 24.5 reduce-scatter.1
